TPU v7x, 128 devices: a whole 4x4x4 slice. The times are simulated.
128 devices in a mesh: tile: 16 (over z_hi, x, core), lag: 8 (over z_lo, y).
Axes of the slice: x: 4, y: 4, z: 4 (z_hi: 2, z_lo: 2; z = z_hi * 2 + z_lo), core: 2. Of those that a mesh axis runs over, the one named last changes fastest.
Arguments:
- history: bfloat16 [16, 128, 384, 512], P('lag', 'tile'), may hold values from -6 to 6
- lag_blocks: bfloat16 [16, 128, 2, 384, 384], P('lag', 'tile'), may hold values from -0.0625 to 0.0625
- self_inverse: bfloat16 [128, 384, 384], P('tile'), may hold values from -0.3125 to 0.3125
- excitation: float32 [128, 384, 512], P('tile'), may hold values from -6 to 6
- pattern: int32 [16, 128, 2], P('lag', 'tile'), may hold values from 0 to 8
- live_counts: int32 [16, 128], P('lag', 'tile'), may hold values from 1 to 2
Outputs:
- traction: bfloat16 [128, 384, 512], P('tile')
- shifted_history: bfloat16 [16, 128, 384, 512], P('lag', 'tile')
All inputs are finite; a program needn't handle non-finite values.
Results may differ from a plain program's by a relative error of at most 0.013.
Values may be sent and summed in bfloat16 or wider, within the bound.
No kernel may reach another device: no remote copies, remote signals or barrier semaphores. Data moves between devices by JAX's collectives and lax.ppermute only.
A program may use at most 128 MiB of HBM per device.

v0:
```python
import jax
import jax.numpy as jnp
from jax import lax
from jax.sharding import PartitionSpec as P

SLOTS = 2
EDGE = 4


def padded(cells, sides, width):
    for axis, dim in sides:
        count = lax.axis_size(axis)
        head = lax.slice_in_dim(cells, 0, width, axis=dim)
        tail = lax.slice_in_dim(cells, cells.shape[dim] - width, cells.shape[dim], axis=dim)
        cells = jnp.concatenate(
            [
                lax.ppermute(tail, axis, [(i, (i + 1) % count) for i in range(count)]),
                cells,
                lax.ppermute(head, axis, [((i + 1) % count, i) for i in range(count)]),
            ],
            axis=dim,
        )
    return cells


def passed_along(array, axis, by):
    length = lax.axis_size(axis)
    pairs = [(i, i + by) for i in range(length) if 0 <= i + by < length]
    return lax.ppermute(array, axis, pairs)


def pick_sources(window, source_index):
    return window[source_index]


def shards(history, lag_blocks, self_inverse, excitation, pattern, live_counts):
    blocks_here = history.shape[1]
    window = padded(history, (("tile", 1),), EDGE)
    positions = jnp.arange(blocks_here, dtype=jnp.int32)
    source_index = positions[None, :, None] + pattern
    sources = jax.vmap(pick_sources)(window, source_index)
    live = jnp.arange(SLOTS, dtype=jnp.int32)[None, None, :] < live_counts[:, :, None]
    sources = sources * live[:, :, :, None, None].astype(sources.dtype)
    partial_field = jnp.einsum(
        "lbsij,lbsjr->bir", lag_blocks, sources, preferred_element_type=jnp.float32
    )
    carried = passed_along(history[-1], "lag", 1)
    field = lax.psum(partial_field.astype(jnp.bfloat16), "lag").astype(jnp.float32)
    residual = (excitation - field).astype(jnp.bfloat16)
    traction = jnp.einsum(
        "bij,bjr->bir", self_inverse, residual, preferred_element_type=jnp.float32
    ).astype(jnp.bfloat16)
    newest = jnp.where(lax.axis_index("lag") == 0, traction, carried)
    shifted_history = jnp.concatenate([newest[None], history[:-1]], axis=0)
    return (traction, shifted_history)


def solution(mesh):
    in_specs = (
        P("lag", "tile", None, None),
        P("lag", "tile", None, None, None),
        P("tile", None, None),
        P("tile", None, None),
        P("lag", "tile", None),
        P("lag", "tile"),
    )
    out_specs = (P("tile", None, None), P("lag", "tile", None, None))
    return jax.shard_map(shards, mesh=mesh, in_specs=in_specs, out_specs=out_specs, check_vma=False)
```

profile of v0, /device:TPU:33, one launch (start us, length us, event | category | flops | bytes accessed | tf_op | source)
XLA Modules:
  0.0 263.7 jit_solution(10920987208944018283)
XLA Ops:
  7.2 0.0 copy-start
  7.2 0.0 copy-start.2
  7.2 0.0 copy-start.3
  7.2 0.0 all-reduce.2.cloned.1.call-start
  7.2 6.2 %fusion.13 = (bf16[2,4,384,512]{3,2,1,0:T(8,128)(2,1)}, bf16[2,4,384,512]{3,2,1,0:T(8,128)(2,1)}) fusion(bf16[2,8,384,512]{3,2,1,0:T(8,128)(2,1)} %param.6), kind=kLoop, calls=%fused_computation.20 | loop fusion | bytes 12582912 | tf_op jit(solution)/shard_map/slice | solution.py:14
  13.5 1.8 collective-permute-start
  15.3 0.0 collective-permute-start.1
  15.3 0.0 copy-done.2
  15.3 0.1 copy.14
  15.4 0.1 reshape.10
  15.5 0.0 copy-done.3
  15.5 0.1 fusion.7
  15.5 34.2 %collective-permute-done = bf16[2,4,384,512]{3,2,1,0:T(8,128)(2,1)} collective-permute-done((bf16[2,4,384,512]{3,2,1,0:T(8,128)(2,1)}, bf16[2,4,384,512]{3,2,1,0:T(8,128)(2,1)}, u32[]{:S(2)}, u32[]{:S(2)}) %collective-permute-start) | collective-permute-done | bytes 3145760 | tf_op jit(solution)/shard_map/ppermute | solution.py:17
  49.8 2.8 %collective-permute-done.1 = bf16[2,4,384,512]{3,2,1,0:T(8,128)(2,1)} collective-permute-done((bf16[2,4,384,512]{3,2,1,0:T(8,128)(2,1)}, bf16[2,4,384,512]{3,2,1,0:T(8,128)(2,1)}, u32[]{:S(2)}, u32[]{:S(2)}) %collective-permute-start.1) | collective-permute-done | bytes 3145760 | tf_op jit(solution)/shard_map/ppermute | solution.py:19
  52.6 10.5 %pad_maximum_fusion = bf16[2,16,384,512]{3,2,1,0:T(8,128)(2,1)} fusion(bf16[2,4,384,512]{3,2,1,0:T(8,128)(2,1)} %collective-permute-done.1, bf16[2,8,384,512]{3,2,1,0:T(8,128)(2,1)} %param.6, bf16[2,4,384,512]{3,2,1,0:T(8,128)(2,1)} %collective-permute-done), kind=kLoop, calls=%fused_computation.1 | loop fusion | flops 12582912 | bytes 25165824 | tf_op jit(solution)/shard_map/concatenate | solution.py:15
  63.1 11.4 %gather_fusion = bf16[32,384,512]{2,1,0:T(8,128)(2,1)} fusion(bf16[2,16,384,512]{3,2,1,0:T(8,128)(2,1)} %pad_maximum_fusion, s32[32]{0:T(128)S(1)} %reshape.10), kind=kCustom, calls=%fused_computation | custom fusion | bytes 25166080 | tf_op jit(solution)/shard_map/vmap()/gather | solution.py:33
  74.5 12.6 %fusion.4 = bf16[8,384,512]{2,1,0:T(8,128)(2,1)} fusion(bf16[2,8,2,384,384]{4,3,2,1,0:T(8,128)(2,1)} %param.7, bf16[2,8,2,384,512]{4,3,2,1,0:T(8,128)(2,1)} %bitcast.24, bf16[2,8,2]{2,1,0:T(8,128)(2,1)S(1)} %fusion.7), kind=kOutput, calls=%fused_computation.9 | convolution fusion | flops 4858576896 | bytes 25165888 | tf_op jit(solution)/shard_map/lbsij,lbsjr->bir/dot_general | solution.py:44
  87.1 0.0 all-reduce.2.cloned.1.call-update
  87.1 6.1 %fusion.12 = (bf16[1,8,384,512]{3,2,1,0:T(8,128)(2,1)}, bf16[1,8,384,512]{3,2,1,0:T(8,128)(2,1)}) fusion(bf16[2,8,384,512]{3,2,1,0:T(8,128)(2,1)} %param.6), kind=kLoop, calls=%fused_computation.19 | loop fusion | bytes 12582912 | tf_op jit(solution)/shard_map/slice | solution.py:47
  93.2 4.7 %copy.22 = bf16[1,8,384,512]{2,3,1,0:T(8,128)(2,1)} copy(bf16[1,8,384,512]{3,2,1,0:T(8,128)(2,1)} %get-tuple-element.6) | data formatting | bytes 6291456
  97.9 3.2 %collective-permute-start.2 = (bf16[8,384,512]{1,2,0:T(8,128)(2,1)}, bf16[8,384,512]{1,2,0:T(8,128)(2,1)}, u32[]{:S(2)}, u32[]{:S(2)}) collective-permute-start(bf16[8,384,512]{1,2,0:T(8,128)(2,1)} %bitcast.25), channel_id=1, source_target_pairs={{0,1},{1,2},{2,3},{3,4},{4,5},{5,6},{6,7},{8,9},{9,10},{10,11},{11... | collective-permute-start | bytes 9437192 | tf_op jit(solution)/shard_map/ppermute | solution.py:29
  101.2 4.6 %copy.23 = bf16[1,8,384,512]{2,3,1,0:T(8,128)(2,1)} copy(bf16[1,8,384,512]{3,2,1,0:T(8,128)(2,1)} %get-tuple-element.7) | data formatting | bytes 6291456
  105.8 124.0 %all-reduce.2.cloned.1.call-done = bf16[8,384,512]{2,1,0:T(8,128)(2,1)} async-done(((bf16[8,384,512]{2,1,0:T(8,128)(2,1)}), bf16[8,384,512]{2,1,0:T(8,128)(2,1)}) %all-reduce.2.cloned.1.call-update) | async-done | bytes 3145744 | tf_op jit(solution)/shard_map/psum | solution.py:48
  229.8 0.0 copy-done
  229.8 7.6 %convert_bitcast_fusion = bf16[8,384,512]{1,2,0:T(8,128)(2,1)} fusion(bf16[8,384,384]{2,1,0:T(8,128)(2,1)S(1)} %copy-done, f32[8,384,512]{2,1,0:T(8,128)} %param.9, bf16[8,384,512]{2,1,0:T(8,128)(2,1)} %all-reduce.2.cloned.1.call-done), kind=kOutput, calls=%fused_computation.11 | convolution fusion | flops 1214251008 | bytes 14942208 | tf_op jit(solution)/shard_map/bij,bjr->bir/dot_general | solution.py:50
  237.4 4.6 %copy.18 = bf16[8,384,512]{2,1,0:T(8,128)(2,1)} copy(bf16[8,384,512]{1,2,0:T(8,128)(2,1)} %convert_bitcast_fusion) | data formatting | bytes 6291456
  242.0 0.0 copy-start.1
  242.0 0.0 collective-permute-done.2
  242.0 2.4 select_bitcast_fusion
  244.4 0.4 copy-done.1
  244.9 3.4 %pad_maximum_fusion.1 = bf16[2,8,384,512]{2,3,1,0:T(8,128)(2,1)} fusion(bf16[1,8,384,512]{2,3,1,0:T(8,128)(2,1)S(1)} %copy-done.1, bf16[1,8,384,512]{2,3,1,0:T(8,128)(2,1)S(1)} %select_bitcast_fusion), kind=kLoop, calls=%fused_computation.4 | loop fusion | flops 3145728 | bytes 12582912 | tf_op jit(solution)/shard_map/concatenate | solution.py:54
  248.2 8.6 %copy.19 = bf16[2,8,384,512]{3,2,1,0:T(8,128)(2,1)} copy(bf16[2,8,384,512]{2,3,1,0:T(8,128)(2,1)} %pad_maximum_fusion.1) | data formatting | bytes 12582912
  (1 shorter events, 0.0 us)
Async XLA Ops:
  7.2 222.6 %copy-start = (bf16[8,384,384]{2,1,0:T(8,128)(2,1)S(1)}, bf16[8,384,384]{2,1,0:T(8,128)(2,1)}, u32[]{:S(2)}) copy-start(bf16[8,384,384]{2,1,0:T(8,128)(2,1)} %param.8) | copy-start | bytes 7077892
  7.2 8.1 %copy-start.2 = (s32[2,8,2]{1,2,0:T(2,128)S(1)}, s32[2,8,2]{1,2,0:T(2,128)}, u32[]{:S(2)}) copy-start(s32[2,8,2]{1,2,0:T(2,128)} %param.10) | copy-start | bytes 388
  7.2 8.3 %copy-start.3 = (s32[2,8]{1,0:T(2,128)S(1)}, s32[2,8]{1,0:T(2,128)}, u32[]{:S(2)}) copy-start(s32[2,8]{1,0:T(2,128)} %param.11) | copy-start | bytes 196
  7.2 222.6 %all-reduce.2.cloned.1.call-start = ((), (), s32[]{:S(2)}) async-start(), calls=%async_computation | async-start | bytes 6291456 | tf_op jit(solution)/shard_map/psum | solution.py:48
  13.5 36.3 %collective-permute-start = (bf16[2,4,384,512]{3,2,1,0:T(8,128)(2,1)}, bf16[2,4,384,512]{3,2,1,0:T(8,128)(2,1)}, u32[]{:S(2)}, u32[]{:S(2)}) collective-permute-start(bf16[2,4,384,512]{3,2,1,0:T(8,128)(2,1)} %get-tuple-element.8), channel_id=1, source_target_pairs={{0,8},{8,16},{16,24},{24,32},{32,40},{40,48},{48,56},{56,64},{64,7... | collective-permute-start | bytes 9437192 | tf_op jit(solution)/shard_map/ppermute | solution.py:17
  15.3 37.3 %collective-permute-start.1 = (bf16[2,4,384,512]{3,2,1,0:T(8,128)(2,1)}, bf16[2,4,384,512]{3,2,1,0:T(8,128)(2,1)}, u32[]{:S(2)}, u32[]{:S(2)}) collective-permute-start(bf16[2,4,384,512]{3,2,1,0:T(8,128)(2,1)} %get-tuple-element.9), channel_id=1, source_target_pairs={{8,0},{16,8},{24,16},{32,24},{40,32},{48,40},{56,48},{64,56},{72,6... | collective-permute-start | bytes 9437192 | tf_op jit(solution)/shard_map/ppermute | solution.py:19
  97.9 144.1 %collective-permute-start.2 = (bf16[8,384,512]{1,2,0:T(8,128)(2,1)}, bf16[8,384,512]{1,2,0:T(8,128)(2,1)}, u32[]{:S(2)}, u32[]{:S(2)}) collective-permute-start(bf16[8,384,512]{1,2,0:T(8,128)(2,1)} %bitcast.25), channel_id=1, source_target_pairs={{0,1},{1,2},{2,3},{3,4},{4,5},{5,6},{6,7},{8,9},{9,10},{10,11},{11... | collective-permute-start | bytes 9437192 | tf_op jit(solution)/shard_map/ppermute | solution.py:29
  242.0 2.8 %copy-start.1 = (bf16[1,8,384,512]{2,3,1,0:T(8,128)(2,1)S(1)}, bf16[1,8,384,512]{2,3,1,0:T(8,128)(2,1)}, u32[]{:S(2)}) copy-start(bf16[1,8,384,512]{2,3,1,0:T(8,128)(2,1)} %copy.23) | copy-start | bytes 9437188
Sparse Core Ops, SparseCore 0:
  87.3 142.4 all-reduce.1
where the time goes:
time: 264 us
  waiting for transfers between devices  161 us (61%)
  local copies, waits for them, and re-layouts  47 us (18%)
  matrix products  20.2 us (8%)
  other arithmetic  16.4 us (6%)
  between operations  14.1 us (5%)
  starting transfers between devices  5.01 us (2%)
    psum x1, waiting for transfers between devices, shards(): lax.psum(partial_field.astype(jnp.bfloat16), 'lag').astype(jnp.float32)  124 us
    ppermute x1, waiting for transfers between devices, padded(): lax.ppermute(tail, axis, [(i, (i + 1) % count) for i in range(count)])  34.2 us
    unnamed x12, local copies, waits for them, and re-layouts  23.1 us
    dot_general x1, matrix products, shards(): jnp.einsum('lbsij,lbsjr->bir', lag_blocks, sources, preferred_element_typ...  12.6 us
    gather x3, local copies, waits for them, and re-layouts, pick_sources(): return window[source_index]  11.6 us
    concatenate x1, other arithmetic, padded(): jnp.concatenate([lax.ppermute(tail, axis, [(i, (i + 1) % count) for i in...  10.5 us
    dot_general x1, matrix products, shards(): jnp.einsum('bij,bjr->bir', self_inverse, residual, preferred_element_type...  7.62 us
    slice x1, local copies, waits for them, and re-layouts, padded(): lax.slice_in_dim(cells, cells.shape[dim] - width, cells.shape[dim], axis=...  6.25 us
  transfers between devices with their start and end apart: 4, of which 3 were waited for; matrix products, arithmetic and copies ran while one was open for 11% of the time, Pallas kernels for 0%

commit v1 on v0

--- a/solution.py
+++ b/solution.py
@@ -5,6 +5,11 @@
 
 SLOTS = 2
 EDGE = 4
+
+
+def gather_and_add(x, axis):
+    pieces = lax.all_gather(x, axis)
+    return jnp.sum(pieces, axis=0)
 
 
 def padded(cells, sides, width):
@@ -45,7 +50,7 @@
         "lbsij,lbsjr->bir", lag_blocks, sources, preferred_element_type=jnp.float32
     )
     carried = passed_along(history[-1], "lag", 1)
-    field = lax.psum(partial_field.astype(jnp.bfloat16), "lag").astype(jnp.float32)
+    field = gather_and_add(partial_field.astype(jnp.bfloat16), "lag").astype(jnp.float32)
     residual = (excitation - field).astype(jnp.bfloat16)
     traction = jnp.einsum(
         "bij,bjr->bir", self_inverse, residual, preferred_element_type=jnp.float32

time: 264 us -> 484 us (1.83)
  waiting for transfers between devices: 161 us -> 331 us
  local copies, waits for them, and re-layouts: 47 us -> 79.7 us
  other arithmetic: 16.4 us -> 31.6 us
    all_gather x0 -> x1, waiting for transfers between devices: none -> 294 us  [gather_and_add(): pieces = lax.all_gather(x, axis)]
    psum x1 -> x0, waiting for transfers between devices: 124 us -> none  [shards(): lax.psum(partial_field.astype(jnp.bfloat16), 'lag').astype(jnp.float32)]
    gather x3 -> x4, local copies, waits for them, and re-layouts: 11.6 us -> 28.2 us  [pick_sources(): return window[source_index]]
    reduce_sum x0 -> x1, other arithmetic: none -> 15.3 us  [gather_and_add(): return jnp.sum(pieces, axis=0)]
    unnamed x12 -> x14, local copies, waits for them, and re-layouts: 23.1 us -> 34.4 us
where the time goes in v1:
time: 484 us; the launch traced here: 483 us
  waiting for transfers between devices  331 us (68%)
  local copies, waits for them, and re-layouts  79.7 us (16%)
  other arithmetic  31.6 us (7%)
  matrix products  21.1 us (4%)
  between operations  14.1 us (3%)
  starting transfers between devices  5.19 us (1%)
    all_gather x1, waiting for transfers between devices, gather_and_add(): pieces = lax.all_gather(x, axis)  294 us
    unnamed x14, local copies, waits for them, and re-layouts  34.4 us
    ppermute x1, waiting for transfers between devices, padded(): lax.ppermute(tail, axis, [(i, (i + 1) % count) for i in range(count)])  34.2 us
    gather x4, local copies, waits for them, and re-layouts, pick_sources(): return window[source_index]  28.2 us
    reduce_sum x1, other arithmetic, gather_and_add(): return jnp.sum(pieces, axis=0)  15.3 us
    dot_general x1, matrix products, shards(): jnp.einsum('lbsij,lbsjr->bir', lag_blocks, sources, preferred_element_typ...  13.6 us
    concatenate x1, other arithmetic, padded(): jnp.concatenate([lax.ppermute(tail, axis, [(i, (i + 1) % count) for i in...  10.5 us
  transfers between devices with their start and end apart: 4, of which 3 were waited for; matrix products, arithmetic and copies ran while one was open for 11% of the time, Pallas kernels for 0%

profile of v1, /device:TPU:33, one launch (start us, length us, event | category | flops | bytes accessed | tf_op | source)
XLA Modules:
  0.0 482.5 jit_solution(7864734396700941871)
XLA Ops:
  7.2 0.0 copy-start
  7.2 0.0 copy-start.2
  7.2 0.0 copy-start.3
  7.2 0.0 all-gather.3.cloned.1.call-start
  7.2 6.2 %fusion.13 = (bf16[2,4,384,512]{3,2,1,0:T(8,128)(2,1)}, bf16[2,4,384,512]{3,2,1,0:T(8,128)(2,1)}) fusion(bf16[2,8,384,512]{3,2,1,0:T(8,128)(2,1)} %param.6), kind=kLoop, calls=%fused_computation.20 | loop fusion | bytes 12582912 | tf_op jit(solution)/shard_map/slice | solution.py:19
  13.5 1.8 collective-permute-start
  15.3 0.0 collective-permute-start.1
  15.3 0.0 copy-done.2
  15.3 0.1 copy.26
  15.4 0.1 reshape.10
  15.5 0.0 copy-done.3
  15.5 0.1 fusion.7
  15.5 34.2 %collective-permute-done = bf16[2,4,384,512]{3,2,1,0:T(8,128)(2,1)} collective-permute-done((bf16[2,4,384,512]{3,2,1,0:T(8,128)(2,1)}, bf16[2,4,384,512]{3,2,1,0:T(8,128)(2,1)}, u32[]{:S(2)}, u32[]{:S(2)}) %collective-permute-start) | collective-permute-done | bytes 3145760 | tf_op jit(solution)/shard_map/ppermute | solution.py:22
  49.8 2.8 collective-permute-done.1
  52.6 10.5 %pad_maximum_fusion = bf16[2,16,384,512]{3,2,1,0:T(8,128)(2,1)} fusion(bf16[2,4,384,512]{3,2,1,0:T(8,128)(2,1)} %collective-permute-done.1, bf16[2,8,384,512]{3,2,1,0:T(8,128)(2,1)} %param.6, bf16[2,4,384,512]{3,2,1,0:T(8,128)(2,1)} %collective-permute-done), kind=kLoop, calls=%fused_computation.1 | loop fusion | flops 12582912 | bytes 25165824 | tf_op jit(solution)/shard_map/concatenate | solution.py:20
  63.1 11.4 %gather_fusion = bf16[32,384,512]{2,1,0:T(8,128)(2,1)} fusion(bf16[2,16,384,512]{3,2,1,0:T(8,128)(2,1)} %pad_maximum_fusion, s32[32]{0:T(128)S(1)} %reshape.10), kind=kCustom, calls=%fused_computation | custom fusion | bytes 25166080 | tf_op jit(solution)/shard_map/vmap()/gather | solution.py:38
  74.5 16.6 %copy.27 = bf16[2,8,2,384,512]{3,4,2,1,0:T(8,128)(2,1)} copy(bf16[2,8,2,384,512]{4,3,2,1,0:T(8,128)(2,1)} %bitcast.25) | data formatting | bytes 25165824 | tf_op jit(solution)/shard_map/vmap()/gather | solution.py:38
  91.1 13.6 %fusion.4 = bf16[8,384,512]{1,2,0:T(8,128)(2,1)} fusion(bf16[2,8,2,384,384]{4,3,2,1,0:T(8,128)(2,1)} %param.7, bf16[2,8,2,384,512]{3,4,2,1,0:T(8,128)(2,1)} %copy.27, bf16[2,8,2]{2,1,0:T(8,128)(2,1)S(1)} %fusion.7), kind=kOutput, calls=%fused_computation.9 | convolution fusion | flops 4839702528 | bytes 25165888 | tf_op jit(solution)/shard_map/lbsij,lbsjr->bir/dot_general | solution.py:49
  104.7 4.7 copy.28
  109.4 0.0 all-gather.3.cloned.1.call-update
  109.5 6.1 %fusion.12 = (bf16[1,8,384,512]{3,2,1,0:T(8,128)(2,1)}, bf16[1,8,384,512]{3,2,1,0:T(8,128)(2,1)}) fusion(bf16[2,8,384,512]{3,2,1,0:T(8,128)(2,1)} %param.6), kind=kLoop, calls=%fused_computation.19 | loop fusion | bytes 12582912 | tf_op jit(solution)/shard_map/slice | solution.py:52
  115.5 4.6 copy.37
  120.2 3.4 collective-permute-start.2
  123.6 6.8 %copy.30 = f32[8,384,512]{1,2,0:T(8,128)} copy(f32[8,384,512]{2,1,0:T(8,128)} %param.9) | data formatting | bytes 12582912 | tf_op args[3]
  130.3 4.7 copy.38
  135.1 293.8 %all-gather.3.cloned.1.call-done = bf16[64,384,512]{2,1,0:T(8,128)(2,1)} async-done(((bf16[8,384,512]{2,1,0:T(8,128)(2,1)}), bf16[64,384,512]{2,1,0:T(8,128)(2,1)}) %all-gather.3.cloned.1.call-update) | async-done | bytes 25165840 | tf_op jit(solution)/shard_map/all_gather | solution.py:11
  428.9 15.3 %reduce_sum.12 = bf16[8,384,512]{2,1,0:T(8,128)(2,1)} reduce(bf16[8,8,384,512]{3,2,1,0:T(8,128)(2,1)} %bitcast.26, bf16[]{:T(256)} %constant.2.clone.1), dimensions={0}, to_apply=%region_0.0 | reduce | flops 11010048 | bytes 28311554 | tf_op jit(solution)/shard_map/reduce_sum | solution.py:12
  444.1 4.6 copy.36
  448.8 0.0 copy-done
  448.8 7.4 %convert_bitcast_fusion = bf16[8,384,512]{1,2,0:T(8,128)(2,1)} fusion(bf16[8,384,384]{2,1,0:T(8,128)(2,1)S(1)} %copy-done, f32[8,384,512]{1,2,0:T(8,128)} %copy.30, bf16[8,384,512]{1,2,0:T(8,128)(2,1)} %copy.36), kind=kOutput, calls=%fused_computation.11 | convolution fusion | flops 1214251008 | bytes 14942208 | tf_op jit(solution)/shard_map/bij,bjr->bir/dot_general | solution.py:55
  456.2 4.6 copy.33
  460.9 0.0 copy-start.1
  460.9 0.0 collective-permute-done.2
  460.9 2.4 select_bitcast_fusion
  463.3 0.4 copy-done.1
  463.7 3.4 pad_maximum_fusion.1
  467.1 8.6 %copy.34 = bf16[2,8,384,512]{3,2,1,0:T(8,128)(2,1)} copy(bf16[2,8,384,512]{2,3,1,0:T(8,128)(2,1)} %pad_maximum_fusion.1) | data formatting | bytes 12582912
  (1 shorter events, 0.0 us)
Async XLA Ops:
  7.2 441.6 %copy-start = (bf16[8,384,384]{2,1,0:T(8,128)(2,1)S(1)}, bf16[8,384,384]{2,1,0:T(8,128)(2,1)}, u32[]{:S(2)}) copy-start(bf16[8,384,384]{2,1,0:T(8,128)(2,1)} %param.8) | copy-start | bytes 7077892
  7.2 8.1 %copy-start.2 = (s32[2,8,2]{1,2,0:T(2,128)S(1)}, s32[2,8,2]{1,2,0:T(2,128)}, u32[]{:S(2)}) copy-start(s32[2,8,2]{1,2,0:T(2,128)} %param.10) | copy-start | bytes 388
  7.2 8.3 %copy-start.3 = (s32[2,8]{1,0:T(2,128)S(1)}, s32[2,8]{1,0:T(2,128)}, u32[]{:S(2)}) copy-start(s32[2,8]{1,0:T(2,128)} %param.11) | copy-start | bytes 196
  7.2 421.7 %all-gather.3.cloned.1.call-start = ((), (), s32[]{:S(2)}) async-start(), calls=%async_computation | async-start | bytes 28311552 | tf_op jit(solution)/shard_map/all_gather | solution.py:11
  13.5 36.3 %collective-permute-start = (bf16[2,4,384,512]{3,2,1,0:T(8,128)(2,1)}, bf16[2,4,384,512]{3,2,1,0:T(8,128)(2,1)}, u32[]{:S(2)}, u32[]{:S(2)}) collective-permute-start(bf16[2,4,384,512]{3,2,1,0:T(8,128)(2,1)} %get-tuple-element.10), channel_id=1, source_target_pairs={{0,8},{8,16},{16,24},{24,32},{32,40},{40,48},{48,56},{56,64},{64,7... | collective-permute-start | bytes 9437192 | tf_op jit(solution)/shard_map/ppermute | solution.py:22
  15.3 37.3 %collective-permute-start.1 = (bf16[2,4,384,512]{3,2,1,0:T(8,128)(2,1)}, bf16[2,4,384,512]{3,2,1,0:T(8,128)(2,1)}, u32[]{:S(2)}, u32[]{:S(2)}) collective-permute-start(bf16[2,4,384,512]{3,2,1,0:T(8,128)(2,1)} %get-tuple-element.11), channel_id=1, source_target_pairs={{8,0},{16,8},{24,16},{32,24},{40,32},{48,40},{56,48},{64,56},{72,6... | collective-permute-start | bytes 9437192 | tf_op jit(solution)/shard_map/ppermute | solution.py:24
  120.2 340.7 %collective-permute-start.2 = (bf16[8,384,512]{1,2,0:T(8,128)(2,1)}, bf16[8,384,512]{1,2,0:T(8,128)(2,1)}, u32[]{:S(2)}, u32[]{:S(2)}) collective-permute-start(bf16[8,384,512]{1,2,0:T(8,128)(2,1)} %bitcast.27), channel_id=1, source_target_pairs={{0,1},{1,2},{2,3},{3,4},{4,5},{5,6},{6,7},{8,9},{9,10},{10,11},{11... | collective-permute-start | bytes 9437192 | tf_op jit(solution)/shard_map/ppermute | solution.py:34
  460.9 2.8 copy-start.1
Sparse Core Ops, SparseCore 0:
  109.6 319.2 all-gather.2
